TPU v7x, 128 devices: a whole 4x4x4 slice. The times are simulated.
128 devices in a mesh: layer: 16 (over y, x), prow: 4 (over z), pcol: 2 (over core).
Axes of the slice: x: 4, y: 4, z: 4, core: 2. Of those that a mesh axis runs over, the one named last changes fastest.
Arguments:
- front: bfloat16 [16, 2048, 32768], P('layer', 'prow', 'pcol'), may hold values from -6 to 6
- pivots: bfloat16 [16, 2, 256, 32768], P('layer', None, 'prow', 'pcol'), may hold values from -0.8984375 to 0.8984375
- inverses: bfloat16 [16, 2, 256, 256], P('layer'), may hold values from -0.1875 to 0.1875
- slab_pattern: int32 [16, 8, 128], P('layer', 'prow', 'pcol'), may hold values 0 or 1
- pivot_pattern: int32 [16, 2, 128], P('layer', None, 'pcol'), may hold values from 0 to 1, as said below
Outputs:
- ancestor: float32 [4, 16, 32, 32768], P('prow', 'layer', None, 'pcol')
- lower: bfloat16 [16, 2048, 512], P('layer', 'prow')
- upper: bfloat16 [16, 256, 32768], P('layer', 'prow', 'pcol')
Inputs may be any that keep to these rules, and one draw needn't show every extreme that they name: `pivot_pattern`: each entry says whether that block of the pivot rows is structurally nonzero. `slab_pattern`: each entry says whether that block of the front rows is structurally nonzero.
All inputs are finite; a program needn't handle non-finite values.
Results may differ from a plain program's by a relative error of at most 0.014.
Values may be sent and summed in bfloat16 or wider, within the bound.
No kernel may reach another device: no remote copies, remote signals or barrier semaphores. Data moves between devices by JAX's collectives and lax.ppermute only.
A program may use at most 192 MiB of HBM per device.

v0:
```python
import jax
import jax.numpy as jnp
from jax import lax
from jax.sharding import PartitionSpec as P


def spread(value, axis, root):
    mine = lax.axis_index(axis) == root
    return lax.psum(jnp.where(mine, value, jnp.zeros_like(value)), axis)


def on_device(front, pivots, inverses, slab_pattern, pivot_pattern):
    block_size = inverses.shape[-1]
    panel_width = 2 * block_size
    row_count = front.shape[1]
    col_count = front.shape[2]
    own_rows = pivots.shape[2]
    masked = (
        front[0].reshape(row_count // block_size, block_size, col_count // block_size, block_size)
        * slab_pattern[0].astype(jnp.bfloat16)[:, None, :, None]
    ).reshape(row_count, col_count)
    pivot_masked = (
        pivots[0].reshape(2, own_rows, col_count // block_size, block_size)
        * pivot_pattern[0].astype(jnp.bfloat16)[:, None, :, None]
    ).reshape(2, own_rows, col_count)
    first_inverse = inverses[0, 0]
    second_inverse = inverses[0, 1]
    row_offset = lax.axis_index("prow") * own_rows
    gathered = lax.all_gather(pivot_masked, "prow", axis=1, tiled=True)
    panel_cols = spread(
        jnp.concatenate(
            [masked[:, :panel_width], gathered[0][:, :panel_width], gathered[1][:, :panel_width]], 0
        ),
        "pcol",
        0,
    )
    front_cols = panel_cols[:row_count]
    pivot_cols = panel_cols[row_count : row_count + block_size]
    second_cols = panel_cols[row_count + block_size :]
    lower_pivot = jnp.dot(
        second_cols[:, :block_size], first_inverse, preferred_element_type=jnp.float32
    ).astype(jnp.bfloat16)
    upper_first = gathered[0]
    upper_second = (
        gathered[1].astype(jnp.float32)
        - jnp.dot(lower_pivot, upper_first, preferred_element_type=jnp.float32)
    ).astype(jnp.bfloat16)
    upper_own = lax.dynamic_slice_in_dim(upper_second, row_offset, own_rows, 0)
    lower_first = jnp.dot(
        front_cols[:, :block_size], first_inverse, preferred_element_type=jnp.float32
    ).astype(jnp.bfloat16)
    carried = (
        front_cols[:, block_size:].astype(jnp.float32)
        - jnp.dot(
            lower_first, pivot_cols[:, block_size:panel_width], preferred_element_type=jnp.float32
        )
    ).astype(jnp.bfloat16)
    lower_second = jnp.dot(carried, second_inverse, preferred_element_type=jnp.float32).astype(
        jnp.bfloat16
    )
    lower_panel = jnp.concatenate([lower_first, lower_second], 1)
    stacked = jnp.concatenate([upper_first, upper_second], 0)
    col_index = lax.axis_index("pcol") * col_count + jnp.arange(col_count, dtype=jnp.int32)
    retained = col_index >= panel_width
    schur_rows = masked.astype(jnp.float32) - jnp.dot(
        lower_panel, stacked, preferred_element_type=jnp.float32
    )
    schur_rows = jnp.where(retained[None, :], schur_rows, jnp.zeros_like(schur_rows))
    summed = lax.psum_scatter(
        schur_rows.astype(jnp.bfloat16), "layer", scatter_dimension=0, tiled=True
    ).astype(jnp.float32)
    ancestor = summed.reshape(1, 1, summed.shape[0], col_count)
    return (ancestor, lower_panel[None], upper_own[None])


def solution(mesh):
    placed = (
        P("layer", "prow", "pcol"),
        P("layer", None, "prow", "pcol"),
        P("layer", None, None, None),
        P("layer", "prow", "pcol"),
        P("layer", None, "pcol"),
    )
    return jax.shard_map(
        on_device,
        mesh=mesh,
        in_specs=placed,
        out_specs=(
            P("prow", "layer", None, "pcol"),
            P("layer", "prow", None),
            P("layer", "prow", "pcol"),
        ),
        check_vma=False,
    )
```

profile of v0, /device:TPU:1, one launch (start us, length us, event | category | flops | bytes accessed | tf_op | source)
XLA Modules:
  0.0 362.8 jit_solution(13036660158709411677)
XLA Ops:
  7.2 0.0 all-gather.2.cloned.1.call-start
  7.2 0.7 convert_bitcast_fusion
  7.9 0.1 broadcast_bitcast_fusion
  8.0 0.1 copy.10
  8.1 4.8 %bitcast_multiply_fusion.1 = bf16[2,64,16384]{2,1,0:T(8,128)(2,1)} fusion(bf16[1,2,64,16384]{3,2,1,0:T(8,128)(2,1)} %param.6, bf16[2,16384]{1,0:T(2,128)(2,1)S(1)} %bitcast.40), kind=kLoop, calls=%fused_computation.9 | loop fusion | flops 2097152 | bytes 8454144 | tf_op jit(solution)/shard_map/mul | solution.py:23
  12.8 0.0 all-gather.2.cloned.1.call-update
  12.9 0.0 all-reduce.2.cloned.1.call-start
  12.9 0.7 convert_bitcast_fusion.1
  13.6 2.7 mul.31
  16.3 10.4 %copy.9 = bf16[64,8,64,256]{3,1,2,0:T(8,128)(2,1)S(1)} copy(bf16[64,8,64,256]{3,2,1,0:T(8,128)(2,1)S(1)} %bitcast.39) | data formatting | bytes 33554432
  26.8 9.7 %bitcast_multiply_fusion = bf16[512,16384]{1,0:T(8,128)(2,1)S(1)} fusion(bf16[512,16384]{1,0:T(8,128)(2,1)S(1)} %bitcast.38, bf16[1,512,16384]{2,1,0:T(8,128)(2,1)} %param.5), kind=kLoop, calls=%fused_computation.6 | loop fusion | flops 8388608 | bytes 50331648 | tf_op jit(solution)/shard_map/mul | solution.py:19
  36.5 0.0 copy-start
  36.5 5.9 %copy-done = bf16[512,16384]{1,0:T(8,128)(2,1)} copy-done((bf16[512,16384]{1,0:T(8,128)(2,1)}, bf16[512,16384]{1,0:T(8,128)(2,1)S(1)}, u32[]{:S(2)}) %copy-start) | copy-done | bytes 16777240
  42.5 0.0 copy-start.2
  42.5 127.9 %all-gather.2.cloned.1.call-done = bf16[2,256,16384]{2,1,0:T(8,128)(2,1)} async-done(((bf16[2,64,16384]{2,1,0:T(8,128)(2,1)}), bf16[2,256,16384]{2,1,0:T(8,128)(2,1)}) %all-gather.2.cloned.1.call-update) | async-done | bytes 16777232 | tf_op jit(solution)/shard_map/all_gather | solution.py:29
  170.4 6.7 %slice_bitcast_fusion.1 = (bf16[256,16384]{1,0:T(8,128)(2,1)S(1)}, bf16[256,16384]{1,0:T(8,128)(2,1)S(1)}) fusion(bf16[2,256,16384]{2,1,0:T(8,128)(2,1)} %all-gather.2.cloned.1.call-done), kind=kLoop, calls=%fused_computation.8 | loop fusion | bytes 33554432 | tf_op jit(solution)/shard_map/squeeze | solution.py:32
  177.1 0.0 copy-start.1
  177.2 3.2 copy-done.1
  180.4 1.2 maximum_select_fusion
  181.6 0.0 all-reduce.2.cloned.1.call-update
  181.6 0.0 reduce-scatter.2.cloned.1.call-start
  181.7 26.6 %all-reduce.2.cloned.1.call-done = bf16[1024,512]{1,0:T(8,128)(2,1)} async-done(((bf16[1024,512]{1,0:T(8,128)(2,1)}), bf16[1024,512]{1,0:T(8,128)(2,1)}) %all-reduce.2.cloned.1.call-update) | async-done | bytes 1048592 | tf_op jit(solution)/shard_map/psum | solution.py:9
  208.3 0.0 copy-done.2
  208.3 9.3 %fusion = bf16[256,16384]{1,0:T(8,128)(2,1)} fusion(bf16[1024,512]{1,0:T(8,128)(2,1)} %all-reduce.2.cloned.1.call-done, bf16[1,2,256,256]{3,2,1,0:T(8,128)(2,1)S(1)} %copy-done.2, bf16[2,256,16384]{2,1,0:T(8,128)(2,1)} %all-gather.2.cloned.1.call-done), kind=kOutput, calls=%fused_computation.2 | convolution fusion | flops 2193686528 | bytes 25427968 | tf_op jit(solution)/shard_map/dot_general | solution.py:46
  217.6 1.2 convolution_convert_fusion.1
  218.8 1.5 convolution_convert_fusion
  220.3 22.0 %select_convert_fusion = bf16[512,16384]{1,0:T(8,128)(2,1)} fusion(bf16[512,16384]{1,0:T(8,128)(2,1)} %copy-done, bf16[256,16384]{1,0:T(8,128)(2,1)} %fusion, bf16[256,16384]{1,0:T(8,128)(2,1)} %copy-done.1, pred[16384]{0:T(1024)(128)(4,1)S(1)} %add_compare_fusion, bf16[512,256]{0,1:T(8,128)(2,1)S(1)} %convolution_convert_fusion, ...), kind=kOutput, calls=%fused_computation | convolution fusion | flops 8658092032 | bytes 50872320 | tf_op jit(solution)/shard_map/dot_general | solution.py:65
  242.2 0.0 reduce-scatter.2.cloned.1.call-update
  242.3 1.0 copy.8
  243.3 3.0 dynamic-slice_bitcast_fusion
  246.4 107.2 %reduce-scatter.2.cloned.1.call-done = bf16[32,16384]{1,0:T(8,128)(2,1)} async-done(((bf16[512,16384]{1,0:T(8,128)(2,1)}), bf16[32,16384]{1,0:T(8,128)(2,1)}) %reduce-scatter.2.cloned.1.call-update) | async-done | bytes 1048592 | tf_op jit(solution)/shard_map/reduce_scatter | solution.py:69
  353.6 2.7 bitcast_convert_fusion
  (5 shorter events, 0.1 us)
Async XLA Ops:
  7.2 163.2 %all-gather.2.cloned.1.call-start = ((), (), s32[]{:S(2)}) async-start(), calls=%async_computation.1 | async-start | bytes 20971520 | tf_op jit(solution)/shard_map/all_gather | solution.py:29
  12.9 195.4 %all-reduce.2.cloned.1.call-start = ((), (), s32[]{:S(2)}) async-start(), calls=%async_computation.2 | async-start | bytes 2097152 | tf_op jit(solution)/shard_map/psum | solution.py:9
  36.5 6.0 %copy-start = (bf16[512,16384]{1,0:T(8,128)(2,1)}, bf16[512,16384]{1,0:T(8,128)(2,1)S(1)}, u32[]{:S(2)}) copy-start(bf16[512,16384]{1,0:T(8,128)(2,1)S(1)} %bitcast_multiply_fusion) | copy-start | bytes 50331652
  42.5 165.8 %copy-start.2 = (bf16[1,2,256,256]{3,2,1,0:T(8,128)(2,1)S(1)}, bf16[1,2,256,256]{3,2,1,0:T(8,128)(2,1)}, u32[]{:S(2)}) copy-start(bf16[1,2,256,256]{3,2,1,0:T(8,128)(2,1)} %param.7) | copy-start | bytes 786436
  177.1 3.2 copy-start.1
  181.6 172.0 %reduce-scatter.2.cloned.1.call-start = ((), (), s32[]{:S(2)}) async-start(), calls=%async_computation.3 | async-start | bytes 17825792 | tf_op jit(solution)/shard_map/reduce_scatter | solution.py:69
Sparse Core Ops, SparseCore 0:
  13.0 157.3 all-gather.1
  181.7 26.5 all-reduce.1
  242.4 111.1 reduce-scatter.1
where the time goes:
time: 363 us
  waiting for transfers between devices  262 us (72%)
  matrix products  33.9 us (9%)
  local copies, waits for them, and re-layouts  33.3 us (9%)
  other arithmetic  19.8 us (5%)
  between operations  13.9 us (4%)
    all_gather x1, waiting for transfers between devices, on_device(): gathered = lax.all_gather(pivot_masked, 'prow', axis=1, tiled=True)  128 us
    reduce_scatter x1, waiting for transfers between devices, on_device(): lax.psum_scatter(schur_rows.astype(jnp.bfloat16), 'layer', scatter_dimens...  107 us
    psum x1, waiting for transfers between devices, spread(): return lax.psum(jnp.where(mine, value, jnp.zeros_like(value)), axis)  26.6 us
    dot_general x1, matrix products, on_device(): jnp.dot(lower_panel, stacked, preferred_element_type=jnp.float32)  22 us
    unnamed x10, local copies, waits for them, and re-layouts  20.7 us
    mul x1, other arithmetic, on_device(): front[0]  9.72 us
    dot_general x1, matrix products, on_device(): jnp.dot(lower_pivot, upper_first, preferred_element_type=jnp.float32)  9.25 us
  transfers between devices with their start and end apart: 3, of which 3 were waited for; matrix products, arithmetic and copies ran while one was open for 8% of the time, Pallas kernels for 0%

commit v1 on v0

--- a/solution.py
+++ b/solution.py
@@ -26,7 +26,32 @@
     first_inverse = inverses[0, 0]
     second_inverse = inverses[0, 1]
     row_offset = lax.axis_index("prow") * own_rows
-    gathered = lax.all_gather(pivot_masked, "prow", axis=1, tiled=True)
+    n_now = lax.axis_size("prow")
+    v1 = lax.axis_index("prow")
+    frames = []
+    part_next, b_next, next_value = (n_now, v1, pivot_masked.shape[1])
+    for dev_j in tuple(range(part_next)):
+        frames.append((dev_j, (dev_j + 1) % part_next))
+    chunks = []
+    for dev_j in tuple(range(part_next)):
+        chunks.append((dev_j, (dev_j - 1) % part_next))
+    gathered = jnp.zeros(
+        (*pivot_masked.shape[:1], part_next * next_value, *pivot_masked.shape[2:]),
+        pivot_masked.dtype,
+    )
+    t_next = then = pivot_masked
+    mat_out = part_next // 2
+    gathered = lax.dynamic_update_slice_in_dim(gathered, pivot_masked, b_next * next_value, axis=1)
+    for w in tuple(range(1, mat_out + 1)):
+        t_next = lax.ppermute(t_next, "prow", frames)
+        gathered = lax.dynamic_update_slice_in_dim(
+            gathered, t_next, (b_next - w) % part_next * next_value, axis=1
+        )
+        if w < part_next - mat_out:
+            then = lax.ppermute(then, "prow", chunks)
+            gathered = lax.dynamic_update_slice_in_dim(
+                gathered, then, (b_next + w) % part_next * next_value, axis=1
+            )
     panel_cols = spread(
         jnp.concatenate(
             [masked[:, :panel_width], gathered[0][:, :panel_width], gathered[1][:, :panel_width]], 0

time: 363 us -> 398 us (1.096)
  local copies, waits for them, and re-layouts: 33.3 us -> 52 us
  waiting for transfers between devices: 262 us -> 271 us
  starting transfers between devices: 0.12 us -> 4.85 us
    ppermute x0 -> x3, waiting for transfers between devices: none -> 138 us  [the longest x2 138 us: on_device(): t_next = lax.ppermute(t_next, 'prow', frames)]
    all_gather x1 -> x0, waiting for transfers between devices: 128 us -> none  [on_device(): gathered = lax.all_gather(pivot_masked, 'prow', axis=1, tiled=True)]
    dynamic_update_slice x0 -> x3, local copies, waits for them, and re-layouts: none -> 13.5 us  [the longest x2 9 us: on_device(): lax.dynamic_update_slice_in_dim(gathered, t_next, (b_next - w) % part_nex...]
    mul x1 -> x0, other arithmetic: 4.78 us -> none  [on_device(): pivots[0].reshape(2, own_rows, col_count // block_size, block_size)]
    ppermute x0 -> x3, starting transfers between devices: none -> 4.59 us  [the longest x2 2.47 us: on_device(): t_next = lax.ppermute(t_next, 'prow', frames)]
    mul x1, other arithmetic: 9.72 us -> 14 us  [on_device(): front[0]]
    unnamed x10 -> x14, local copies, waits for them, and re-layouts: 20.7 us -> 21.1 us
  transfers between devices with their start and end apart: 3 -> 5, of which waited for: 3 -> 4; matrix products, arithmetic and copies ran while one was open for 8% -> 12% of each run, Pallas kernels for 0% -> 0%
where the time goes in v1:
time: 398 us
  waiting for transfers between devices  271 us (68%)
  local copies, waits for them, and re-layouts  52 us (13%)
  matrix products  34 us (9%)
  other arithmetic  21.6 us (5%)
  between operations  14.2 us (4%)
  starting transfers between devices  4.85 us (1%)
    ppermute x2, waiting for transfers between devices, on_device(): t_next = lax.ppermute(t_next, 'prow', frames)  138 us
    reduce_scatter x1, waiting for transfers between devices, on_device(): lax.psum_scatter(schur_rows.astype(jnp.bfloat16), 'layer', scatter_dimens...  107 us
    psum x1, waiting for transfers between devices, spread(): return lax.psum(jnp.where(mine, value, jnp.zeros_like(value)), axis)  25.9 us
    dot_general x1, matrix products, on_device(): jnp.dot(lower_panel, stacked, preferred_element_type=jnp.float32)  21.9 us
    unnamed x14, local copies, waits for them, and re-layouts  21.1 us
    mul x1, other arithmetic, on_device(): front[0]  14 us
    dot_general x1, matrix products, on_device(): jnp.dot(lower_pivot, upper_first, preferred_element_type=jnp.float32)  9.32 us
    dynamic_update_slice x2, local copies, waits for them, and re-layouts, on_device(): lax.dynamic_update_slice_in_dim(gathered, t_next, (b_next - w) % part_nex...  9 us
  transfers between devices with their start and end apart: 5, of which 4 were waited for; matrix products, arithmetic and copies ran while one was open for 12% of the time, Pallas kernels for 0%

profile of v1, /device:TPU:1, one launch (start us, length us, event | category | flops | bytes accessed | tf_op | source)
XLA Modules:
  0.0 397.5 jit_solution(14270966305455092176)
XLA Ops:
  7.2 0.0 all-reduce.2.cloned.1.call-start
  7.2 0.7 convert_bitcast_fusion
  7.9 0.1 broadcast_bitcast_fusion
  8.0 0.1 copy.10
  8.1 1.2 broadcast_in_dim.27
  9.3 1.0 copy-done.2
  10.3 3.1 constant_dynamic-update-slice_fusion.3
  13.3 2.5 collective-permute-start
  15.8 2.1 collective-permute-start.1
  17.9 6.3 %mul.41 = bf16[2,256,64,256]{3,2,1,0:T(8,128)(2,1)} broadcast(bf16[2,64]{1,0:T(2,128)(2,1)S(1)} %convert_bitcast_fusion.1), dimensions={0,2} | broadcast | bytes 16777472 | tf_op jit(solution)/shard_map/mul | solution.py:19
  24.2 15.8 %copy.9 = bf16[64,8,64,256]{3,1,2,0:T(8,128)(2,1)S(1)} copy(bf16[64,8,64,256]{3,2,1,0:T(8,128)(2,1)} %bitcast.40) | data formatting | bytes 33554432
  40.0 68.5 %collective-permute-done = bf16[2,64,16384]{2,1,0:T(8,128)(2,1)} collective-permute-done((bf16[2,64,16384]{2,1,0:T(8,128)(2,1)}, bf16[2,64,16384]{2,1,0:T(8,128)(2,1)}, u32[]{:S(2)}, u32[]{:S(2)}) %collective-permute-start) | collective-permute-done | bytes 4194336 | tf_op jit(solution)/shard_map/ppermute | solution.py:46
  108.5 14.0 %bitcast_multiply_fusion = bf16[512,16384]{1,0:T(8,128)(2,1)} fusion(bf16[512,16384]{1,0:T(8,128)(2,1)S(1)} %bitcast.39, bf16[1,512,16384]{2,1,0:T(8,128)(2,1)} %param.5), kind=kLoop, calls=%fused_computation.4 | loop fusion | flops 8388608 | bytes 50331648 | tf_op jit(solution)/shard_map/mul | solution.py:19
  122.5 4.5 %constant_dynamic-update-slice_fusion.2 = bf16[2,256,16384]{2,1,0:T(8,128)(2,1)} fusion(bf16[2,256,16384]{2,1,0:T(8,128)(2,1)} %copy-done, bf16[2,64,16384]{2,1,0:T(8,128)(2,1)} %collective-permute-done, s32[]{:T(128)S(6)} %select_n.43), kind=kLoop, calls=%fused_computation.35 | loop fusion | bytes 8388612 | tf_op jit(solution)/shard_map/dynamic_update_slice | solution.py:47
  127.0 4.5 %constant_dynamic-update-slice_fusion.1 = bf16[2,256,16384]{2,1,0:T(8,128)(2,1)} fusion(bf16[2,256,16384]{2,1,0:T(8,128)(2,1)} %constant_dynamic-update-slice_fusion.2, bf16[2,64,16384]{2,1,0:T(8,128)(2,1)} %collective-permute-done.1, s32[]{:T(128)S(6)} %select_n.45), kind=kLoop, calls=%fused_computation.34 | loop fusion | bytes 8388612 | tf_op jit(solution)/shard_map/dynamic_update_slice | solution.py:52
  131.5 69.4 %collective-permute-done.2 = bf16[2,64,16384]{2,1,0:T(8,128)(2,1)} collective-permute-done((bf16[2,64,16384]{2,1,0:T(8,128)(2,1)}, bf16[2,64,16384]{2,1,0:T(8,128)(2,1)}, u32[]{:S(2)}, u32[]{:S(2)}) %collective-permute-start.2) | collective-permute-done | bytes 4194336 | tf_op jit(solution)/shard_map/ppermute | solution.py:46
  200.9 4.5 %constant_dynamic-update-slice_fusion = bf16[2,256,16384]{2,1,0:T(8,128)(2,1)} fusion(bf16[2,256,16384]{2,1,0:T(8,128)(2,1)} %constant_dynamic-update-slice_fusion.1, bf16[2,64,16384]{2,1,0:T(8,128)(2,1)} %collective-permute-done.2, s32[]{:T(128)S(6)} %select_n.47), kind=kLoop, calls=%fused_computation.33 | loop fusion | bytes 8388612 | tf_op jit(solution)/shard_map/dynamic_update_slice | solution.py:47
  205.4 6.8 %slice_bitcast_fusion.1 = (bf16[256,16384]{1,0:T(8,128)(2,1)S(1)}, bf16[256,16384]{1,0:T(8,128)(2,1)S(1)}) fusion(bf16[2,256,16384]{2,1,0:T(8,128)(2,1)} %constant_dynamic-update-slice_fusion), kind=kLoop, calls=%fused_computation.7 | loop fusion | bytes 33554432 | tf_op jit(solution)/shard_map/squeeze | solution.py:57
  212.3 3.2 copy-done.1
  215.5 1.2 maximum_select_fusion
  216.7 0.0 all-reduce.2.cloned.1.call-update
  216.7 0.2 reduce-scatter.2.cloned.1.call-start
  216.9 25.9 %all-reduce.2.cloned.1.call-done = bf16[1024,512]{1,0:T(8,128)(2,1)} async-done(((bf16[1024,512]{1,0:T(8,128)(2,1)}), bf16[1024,512]{1,0:T(8,128)(2,1)}) %all-reduce.2.cloned.1.call-update) | async-done | bytes 1048592 | tf_op jit(solution)/shard_map/psum | solution.py:9
  242.8 9.3 %subtract_convert_fusion = bf16[256,16384]{1,0:T(8,128)(2,1)} fusion(bf16[1024,512]{1,0:T(8,128)(2,1)} %all-reduce.2.cloned.1.call-done, bf16[1,2,256,256]{3,2,1,0:T(8,128)(2,1)S(1)} %copy-done.3, bf16[2,256,16384]{2,1,0:T(8,128)(2,1)} %constant_dynamic-update-slice_fusion), kind=kOutput, calls=%fused_computation.5 | convolution fusion | flops 2193686528 | bytes 25427968 | tf_op jit(solution)/shard_map/dot_general | solution.py:71
  252.1 1.2 convolution_convert_fusion.1
  253.4 1.5 convolution_convert_fusion
  254.9 21.9 %select_convert_fusion = bf16[512,16384]{1,0:T(8,128)(2,1)} fusion(bf16[512,16384]{1,0:T(8,128)(2,1)} %bitcast_multiply_fusion, bf16[256,16384]{1,0:T(8,128)(2,1)} %subtract_convert_fusion, bf16[256,16384]{1,0:T(8,128)(2,1)} %copy-done.1, pred[16384]{0:T(1024)(128)(4,1)S(1)} %add_compare_fusion, bf16[512,256]{0,1:T(8,128)(2,1)S(1)} %convolution_convert_fusion, ...), kind=kOutput, calls=%fused_computation | convolution fusion | flops 8658092032 | bytes 50872320 | tf_op jit(solution)/shard_map/dot_general | solution.py:90
  276.8 0.0 reduce-scatter.2.cloned.1.call-update
  276.9 1.0 copy.8
  277.9 3.0 dynamic-slice_bitcast_fusion
  280.9 107.1 %reduce-scatter.2.cloned.1.call-done = bf16[32,16384]{1,0:T(8,128)(2,1)} async-done(((bf16[512,16384]{1,0:T(8,128)(2,1)}), bf16[32,16384]{1,0:T(8,128)(2,1)}) %reduce-scatter.2.cloned.1.call-update) | async-done | bytes 1048592 | tf_op jit(solution)/shard_map/reduce_scatter | solution.py:94
  388.0 2.7 bitcast_convert_fusion
  (17 shorter events, 0.1 us)
Async XLA Ops:
  7.2 10.8 %copy-start.4 = (s32[1,2,64]{2,1,0:T(2,128)S(1)}, s32[1,2,64]{2,1,0:T(2,128)}, u32[]{:S(2)}) copy-start(s32[1,2,64]{2,1,0:T(2,128)} %param.8) | copy-start | bytes 1540
  7.2 235.6 %all-reduce.2.cloned.1.call-start = ((), (), s32[]{:S(2)}) async-start(), calls=%async_computation.1 | async-start | bytes 2097152 | tf_op jit(solution)/shard_map/psum | solution.py:9
  8.1 2.2 copy-start.2
  13.3 26.7 %copy-start = (bf16[2,256,16384]{2,1,0:T(8,128)(2,1)}, bf16[2,256,16384]{2,1,0:T(8,128)(2,1)S(1)}, u32[]{:S(2)}) copy-start(bf16[2,256,16384]{2,1,0:T(8,128)(2,1)S(1)} %get-tuple-element.6) | copy-start | bytes 50331652
  13.3 95.2 %collective-permute-start = (bf16[2,64,16384]{2,1,0:T(8,128)(2,1)}, bf16[2,64,16384]{2,1,0:T(8,128)(2,1)}, u32[]{:S(2)}, u32[]{:S(2)}) collective-permute-start(bf16[2,64,16384]{2,1,0:T(8,128)(2,1)} %get-tuple-element.7), channel_id=1, source_target_pairs={{0,2},{2,4},{4,6},{6,0},{1,3},{3,5},{5,7},{7,1},{8,10},{10,12},{12... | collective-permute-start | bytes 12582920 | tf_op jit(solution)/shard_map/ppermute | solution.py:46
  15.8 111.2 %collective-permute-start.1 = (bf16[2,64,16384]{2,1,0:T(8,128)(2,1)}, bf16[2,64,16384]{2,1,0:T(8,128)(2,1)}, u32[]{:S(2)}, u32[]{:S(2)}) collective-permute-start(bf16[2,64,16384]{2,1,0:T(8,128)(2,1)} %get-tuple-element.7), channel_id=1, source_target_pairs={{0,6},{2,0},{4,2},{6,4},{1,7},{3,1},{5,3},{7,5},{8,14},{10,8},{12,... | collective-permute-start | bytes 12582920 | tf_op jit(solution)/shard_map/ppermute | solution.py:51
  108.5 92.4 %collective-permute-start.2 = (bf16[2,64,16384]{2,1,0:T(8,128)(2,1)}, bf16[2,64,16384]{2,1,0:T(8,128)(2,1)}, u32[]{:S(2)}, u32[]{:S(2)}) collective-permute-start(bf16[2,64,16384]{2,1,0:T(8,128)(2,1)} %collective-permute-done), channel_id=1, source_target_pairs={{0,2},{2,4},{4,6},{6,0},{1,3},{3,5},{5,7},{7,1},{8,10},{10,12},{12... | collective-permute-start | bytes 12582920 | tf_op jit(solution)/shard_map/ppermute | solution.py:46
  205.4 10.1 %slice-start = ((bf16[512,16384]{1,0:T(8,128)(2,1)}), bf16[512,512]{1,0:T(8,128)(2,1)S(1)}, s32[]{:S(2)}) async-start(bf16[512,16384]{1,0:T(8,128)(2,1)} %bitcast_multiply_fusion), calls=%async_computation.3 | async-start | bytes 1048576 | tf_op jit(solution)/shard_map/slice | solution.py:57
  205.4 37.4 %copy-start.3 = (bf16[1,2,256,256]{3,2,1,0:T(8,128)(2,1)S(1)}, bf16[1,2,256,256]{3,2,1,0:T(8,128)(2,1)}, u32[]{:S(2)}) copy-start(bf16[1,2,256,256]{3,2,1,0:T(8,128)(2,1)} %param.7) | copy-start | bytes 786436
  212.2 3.2 copy-start.1
  216.7 171.3 %reduce-scatter.2.cloned.1.call-start = ((), (), s32[]{:S(2)}) async-start(), calls=%async_computation.2 | async-start | bytes 17825792 | tf_op jit(solution)/shard_map/reduce_scatter | solution.py:94
Sparse Core Ops, SparseCore 0:
  216.8 25.9 all-reduce.1
  276.9 111.0 reduce-scatter.1
